TPU v7x, 128 devices: a whole 4x4x4 slice. The times are simulated.
128 devices in a mesh: seq: 32 (over z, x, y_lo), type: 4 (over y_hi, core).
Axes of the slice: x: 4, y: 4 (y_hi: 2, y_lo: 2; y = y_hi * 2 + y_lo), z: 4, core: 2. Of those that a mesh axis runs over, the one named last changes fastest.
Arguments:
- tokens: bfloat16 [17408, 1024], P(('seq', 'type')), may hold values from -60 to 60
- shift_scale: float32 [2, 1024], replicated, may hold values from -0.8 to 0.8
- branch_gate: float32 [1024], replicated, may hold values from 0.25 to 1.75
- final_gain: float32 [1024], replicated, may hold values from 0.5 to 1.5
- w_qkv: bfloat16 [3, 1024, 1024], P(None, None, 'type'), may hold values from -1 to 1
- w_out: bfloat16 [1024, 1024], P('type'), may hold values from -0.375 to 0.375
- type_ids: int32 [17408, 1], P(('seq', 'type')), may hold values from 0 to 7; in each aligned block of 136 rows (0 to 135, 136 to 271, ...) at most 51 rows name the same one
- head_w1: bfloat16 [8, 1024, 1024], P('type'), may hold values from -0.1875 to 0.1875
- head_b1: bfloat16 [8, 1024], P('type'), may hold values from -3 to 3
- head_w2: bfloat16 [8, 1024, 16], P('type'), may hold values from -0.1875 to 0.1875
Outputs:
- updated: bfloat16 [17408, 1024], P(('seq', 'type'))
- head_out: float32 [17408, 16], P(('seq', 'type'))
Inputs may be any that keep to these rules, and one draw needn't show every extreme that they name: `type_ids`: among the 136 tokens of one device no type occurs more than 51 times; some type occurs exactly 51 times on some devices.
All inputs are finite; a program needn't handle non-finite values.
Results may differ from a plain program's by a relative error of at most 0.014.
Values may be sent and summed in bfloat16 or wider, within the bound.
No kernel may reach another device: no remote copies, remote signals or barrier semaphores. Data moves between devices by JAX's collectives and lax.ppermute only.
A program may use at most 192 MiB of HBM per device.

v0:
```python
import jax
import jax.numpy as jnp
from jax import lax
from jax.sharding import PartitionSpec as P

HD = 64


def rms_normalize(values):
    squares = jnp.mean(values * values, axis=-1, keepdims=True)
    return values * lax.rsqrt(squares + 1e-06)


def absorb_block(state, query_heads, key_heads, value_heads):
    largest, totals, numer = state
    scores = jnp.einsum(
        "qhd,khd->hqk", query_heads, key_heads, preferred_element_type=jnp.float32
    ) * HD ** (-0.5)
    newmax = jnp.maximum(largest, jnp.max(scores, axis=-1))
    decay = jnp.exp(largest - newmax)
    weights = jnp.exp(scores - newmax[:, :, None])
    totals = totals * decay + jnp.sum(weights, axis=-1)
    update = jnp.einsum(
        "hqk,khd->qhd",
        weights.astype(jnp.bfloat16),
        value_heads,
        preferred_element_type=jnp.float32,
    )
    numer = numer * jnp.transpose(decay)[:, :, None] + update
    return (newmax, totals, numer)


def apply_heads(feature_slots, first_w, first_b, second_w):
    hidden = jnp.einsum(
        "...tcd,tdh->...tch", feature_slots, first_w, preferred_element_type=jnp.float32
    )
    hidden = jax.nn.gelu(hidden + first_b.astype(jnp.float32)[:, None, :]).astype(jnp.bfloat16)
    return jnp.einsum("...tch,tho->...tco", hidden, second_w, preferred_element_type=jnp.float32)


def body(
    tokens, shift_scale, branch_gate, final_gain, w_qkv, w_out, type_ids, head_w1, head_b1, head_w2
):
    inputs = tokens.astype(jnp.float32)
    modulated = (rms_normalize(inputs) * (1.0 + shift_scale[1]) + shift_scale[0]).astype(
        jnp.bfloat16
    )
    projected = jnp.einsum(
        "rd,ide->ire",
        lax.all_gather(modulated, "type", axis=0, tiled=True),
        w_qkv,
        preferred_element_type=jnp.float32,
    ).astype(jnp.bfloat16)
    queries = projected[0]
    local_keys = projected[1]
    local_values = projected[2]
    query_count = queries.shape[0]
    width = queries.shape[1]
    local_heads = width // HD
    query_heads = queries.reshape(query_count, local_heads, HD)
    initial = (
        jnp.full((local_heads, query_count), -1e30, jnp.float32),
        jnp.zeros((local_heads, query_count), jnp.float32),
        jnp.zeros((query_count, local_heads, HD), jnp.float32),
    )
    running = initial
    key_part = lax.all_gather(local_keys, "seq", axis=0, tiled=True)
    value_part = lax.all_gather(local_values, "seq", axis=0, tiled=True)
    row_total = key_part.shape[0]
    key_blocks = key_part.reshape(row_total // 512, 512, local_heads, HD)
    value_blocks = value_part.reshape(row_total // 512, 512, local_heads, HD)

    def advance(state, pair):
        return (absorb_block(state, query_heads, pair[0], pair[1]), None)

    running, unused = lax.scan(advance, running, (key_blocks, value_blocks))
    largest, totals, numer = running
    attended = (
        (numer / jnp.transpose(totals)[:, :, None]).astype(jnp.bfloat16).reshape(query_count, width)
    )
    mixed = lax.psum_scatter(
        jnp.dot(attended, w_out, preferred_element_type=jnp.float32),
        "type",
        scatter_dimension=0,
        tiled=True,
    )
    updated = (inputs + branch_gate * mixed).astype(jnp.bfloat16)
    final = (rms_normalize(updated.astype(jnp.float32)) * final_gain).astype(jnp.bfloat16)
    owned = head_w1.shape[0]
    owners = lax.axis_size("type")
    kinds_all = owned * owners
    capacity = 3 * tokens.shape[0] // 8
    kinds = type_ids[:, 0]
    onehot = (kinds[:, None] == jnp.arange(kinds_all, dtype=jnp.int32)[None, :]).astype(jnp.int32)
    ranks = jnp.sum((jnp.cumsum(onehot, axis=0) - onehot) * onehot, axis=1)
    slots = kinds * capacity + ranks
    slot_ids = jnp.arange(kinds_all * capacity, dtype=jnp.int32)
    dispatch = (slot_ids[:, None] == slots[None, :]).astype(jnp.bfloat16)
    packed = jnp.dot(dispatch, final, preferred_element_type=jnp.float32).astype(jnp.bfloat16)
    packed = packed.reshape(kinds_all, capacity, final.shape[1])
    first_w, first_b, second_w = (
        lax.all_gather(head_w1, "type", axis=0, tiled=True),
        lax.all_gather(head_b1, "type", axis=0, tiled=True),
        lax.all_gather(head_w2, "type", axis=0, tiled=True),
    )
    answers = apply_heads(packed, first_w, first_b, second_w)
    answers = answers.reshape(kinds_all * capacity, head_w2.shape[2])
    gather_back = (slots[:, None] == slot_ids[None, :]).astype(jnp.float32)
    head_out = jnp.dot(
        gather_back, answers, precision=lax.Precision.HIGHEST, preferred_element_type=jnp.float32
    )
    return (updated, head_out)


def solution(mesh):
    in_specs = (
        P(("seq", "type"), None),
        P(),
        P(),
        P(),
        P(None, None, "type"),
        P("type", None),
        P(("seq", "type"), None),
        P("type", None, None),
        P("type", None),
        P("type", None, None),
    )
    out_specs = (P(("seq", "type"), None), P(("seq", "type"), None))
    return jax.shard_map(body, mesh=mesh, in_specs=in_specs, out_specs=out_specs, check_vma=False)
```

profile of v0, /device:TPU:1, one launch (start us, length us, event | category | flops | bytes accessed | tf_op | source)
XLA Modules:
  0.0 957.8 jit_solution(635125774649194052)
XLA Ops:
  11.1 24.9 %all-gather.8.cloned.1.call-done = bf16[544,1024]{1,0:T(8,128)(2,1)} async-done(((bf16[136,1024]{1,0:T(8,128)(2,1)}), bf16[544,1024]{1,0:T(8,128)(2,1)}) %all-gather.8.cloned.1.call-update) | async-done | bytes 1114128 | tf_op jit(solution)/shard_map/all_gather | solution.py:50
  40.1 196.5 %all-gather.12.cloned.1.call-done = bf16[1,17408,256]{2,1,0:T(8,128)(2,1)} async-done(((bf16[1,544,256]{2,1,0:T(8,128)(2,1)}), bf16[1,17408,256]{2,1,0:T(8,128)(2,1)}) %all-gather.12.cloned.1.call-update) | async-done | bytes 8912912 | tf_op jit(solution)/shard_map/all_gather | solution.py:67
  236.6 25.9 %reshape.77 = bf16[34,512,4,64]{3,2,1,0:T(4,128)(2,1)} reshape(bf16[1,17408,256]{2,1,0:T(8,128)(2,1)} %all-gather.12.cloned.1.call-done) | data formatting | bytes 17825792 | tf_op jit(solution)/shard_map/reshape | solution.py:70
  262.5 25.6 %copy.24 = bf16[34,512,4,64]{1,3,2,0:T(8,128)(2,1)} copy(bf16[34,512,4,64]{3,2,1,0:T(4,128)(2,1)} %reshape.77) | data formatting | bytes 17825792
  288.2 150.6 %all-gather.14.cloned.1.call-done = bf16[1,17408,256]{2,1,0:T(8,128)(2,1)} async-done(((bf16[1,544,256]{2,1,0:T(8,128)(2,1)}), bf16[1,17408,256]{2,1,0:T(8,128)(2,1)}) %all-gather.14.cloned.1.call-update) | async-done | bytes 8912912 | tf_op jit(solution)/shard_map/all_gather | solution.py:68
  438.8 25.9 %reshape.78 = bf16[34,512,4,64]{3,2,1,0:T(4,128)(2,1)} reshape(bf16[1,17408,256]{2,1,0:T(8,128)(2,1)} %all-gather.14.cloned.1.call-done) | data formatting | bytes 17825792 | tf_op jit(solution)/shard_map/reshape | solution.py:71
  464.7 25.6 %copy.25 = bf16[34,512,4,64]{1,3,2,0:T(8,128)(2,1)} copy(bf16[34,512,4,64]{3,2,1,0:T(4,128)(2,1)} %reshape.78) | data formatting | bytes 17825792
  490.3 298.6 %while.15 = (s32[]{:T(128)}, f32[4,544]{1,0:T(4,128)S(1)}, f32[4,544]{1,0:T(4,128)S(1)}, f32[544,4,64]{0,2,1:T(8,128)S(1)}, bf16[34,512,4,64]{1,3,2,0:T(8,128)(2...) while((s32[]{:T(128)}, f32[4,544]{1,0:T(4,128)S(1)}, ...), condition=%wide.region_4.5_spmd.clone, body=%wide.region_1.4_spmd.clone.sunk | while | flops 294556416 | bytes 33252484 | solution.py:76
  490.3 3.8 bitcast_reduce_fusion.2
  507.9 3.8 bitcast_reduce_fusion.2
  516.7 3.8 bitcast_reduce_fusion.2
  525.5 3.8 bitcast_reduce_fusion.2
  551.9 3.8 bitcast_reduce_fusion.2
  578.2 3.8 bitcast_reduce_fusion.2
  604.5 3.8 bitcast_reduce_fusion.2
  613.3 3.8 bitcast_reduce_fusion.2
  639.7 3.8 bitcast_reduce_fusion.2
  648.4 3.8 bitcast_reduce_fusion.2
  666.0 3.8 bitcast_reduce_fusion.2
  792.4 11.0 %all-gather.2 = bf16[4,2,1024]{2,1,0:T(2,128)(2,1)S(1)} all-gather(bf16[1,2,1024]{2,1,0:T(2,128)(2,1)S(1)} %bitcast.83), channel_id=1, replica_groups=mesh['seq'=32,'type'=4] {'type'}, dimensions={0}, use_global_device_ids=true | all-gather | bytes 20480 | tf_op jit(solution)/shard_map/all_gather | solution.py:103
  803.5 7.4 all_gather.23
  811.0 20.2 %reduce-scatter.2.cloned.1.call-done = f32[136,1024]{1,0:T(8,128)} async-done(((f32[544,1024]{1,0:T(8,128)}), f32[136,1024]{1,0:T(8,128)}) %reduce-scatter.2.cloned.1.call-update) | async-done | bytes 557072 | tf_op jit(solution)/shard_map/reduce_scatter | solution.py:81
  833.3 109.4 %all-gather.10.cloned.1.call-done = bf16[8,1024,1024]{2,1,0:T(8,128)(2,1)} async-done(((bf16[2,1024,1024]{2,1,0:T(8,128)(2,1)}), bf16[8,1024,1024]{2,1,0:T(8,128)(2,1)}) %all-gather.10.cloned.1.call-update) | async-done | bytes 16777232 | tf_op jit(solution)/shard_map/all_gather | solution.py:102
  942.7 7.6 fusion.32
  (321 shorter events, 270.3 us)
Async XLA Ops:
  7.2 28.8 %copy-start = (bf16[3,1024,256]{2,1,0:T(8,128)(2,1)S(1)}, bf16[3,1024,256]{2,1,0:T(8,128)(2,1)}, u32[]{:S(2)}) copy-start(bf16[3,1024,256]{2,1,0:T(8,128)(2,1)} %param.16) | copy-start | bytes 4718596
  7.2 28.7 %all-gather.8.cloned.1.call-start = ((), (), s32[]{:S(2)}) async-start(), calls=%async_computation.1 | async-start | bytes 1392640 | tf_op jit(solution)/shard_map/all_gather | solution.py:50
  11.0 225.6 %all-gather.12.cloned.1.call-start = ((), (), s32[]{:S(2)}) async-start(), calls=%async_computation.4 | async-start | bytes 9191424 | tf_op jit(solution)/shard_map/all_gather | solution.py:67
  39.1 399.7 %all-gather.14.cloned.1.call-start = ((), (), s32[]{:S(2)}) async-start(), calls=%async_computation.5 | async-start | bytes 9191424 | tf_op jit(solution)/shard_map/all_gather | solution.py:68
  39.8 791.4 %reduce-scatter.2.cloned.1.call-start = ((), (), s32[]{:S(2)}) async-start(), calls=%async_computation.2 | async-start | bytes 2785280 | tf_op jit(solution)/shard_map/reduce_scatter | solution.py:81
  490.3 298.7 %copy-start.5 = (bf16[256,1024]{1,0:T(8,128)(2,1)S(1)}, bf16[256,1024]{1,0:T(8,128)(2,1)}, u32[]{:S(2)}) copy-start(bf16[256,1024]{1,0:T(8,128)(2,1)} %param.17) | copy-start | bytes 1572868
  494.2 3.7 copy-start.2
  529.3 3.7 copy-start.2
  555.6 3.7 copy-start.2
  590.7 3.7 copy-start.2
  617.1 3.7 copy-start.2
  625.9 3.7 copy-start.2
  652.2 3.7 copy-start.2
  678.6 3.7 copy-start.2
  713.7 3.7 copy-start.2
  740.0 3.7 copy-start.2
  748.8 3.7 copy-start.2
  789.0 14.4 %copy-start.6 = (bf16[2,1024,16]{1,2,0:T(8,128)(2,1)S(1)}, bf16[2,1024,16]{1,2,0:T(8,128)(2,1)}, u32[]{:S(2)}) copy-start(bf16[2,1024,16]{1,2,0:T(8,128)(2,1)} %param.21) | copy-start | bytes 196612
  789.1 42.2 %copy-start.3 = (bf16[136,1024]{1,0:T(8,128)(2,1)S(1)}, bf16[136,1024]{1,0:T(8,128)(2,1)}, u32[]{:S(2)}) copy-start(bf16[136,1024]{1,0:T(8,128)(2,1)} %param.12) | copy-start | bytes 835588
  789.1 42.2 %copy-start.8 = (f32[1024]{0:T(1024)S(1)}, f32[1024]{0:T(1024)}, u32[]{:S(2)}) copy-start(f32[1024]{0:T(1024)} %param.14) | copy-start | bytes 12292
  790.9 41.6 %copy-start.9 = (f32[1024]{0:T(1024)S(1)}, f32[1024]{0:T(1024)}, u32[]{:S(2)}) copy-start(f32[1024]{0:T(1024)} %param.15) | copy-start | bytes 12292
  791.0 151.7 %all-gather.10.cloned.1.call-start = ((), (), s32[]{:S(2)}) async-start(), calls=%async_computation.3 | async-start | bytes 20971520 | tf_op jit(solution)/shard_map/all_gather | solution.py:102
  832.5 117.8 %copy-start.4 = (bf16[136,1024]{1,0:T(8,128)(2,1)}, bf16[136,1024]{1,0:T(8,128)(2,1)S(1)}, u32[]{:S(2)}) copy-start(bf16[136,1024]{1,0:T(8,128)(2,1)S(1)} %get-tuple-element.104) | copy-start | bytes 835588
  942.7 8.6 copy-start.1
  (25 other events, 90.6 us)
Sparse Core Ops, SparseCore 0:
  11.1 24.7 all-gather.7
  39.2 197.3 all-gather.11
  238.8 199.9 all-gather.13
  791.1 40.1 reduce-scatter.1
  832.8 109.7 all-gather.9
where the time goes:
time: 962 us; the launch traced here: 958 us
  waiting for transfers between devices  503 us (52%)
  matrix products  264 us (27%)
  local copies, waits for them, and re-layouts  106 us (11%)
  other arithmetic  50.4 us (5%)
  blocking collectives  18.4 us (2%)
  between operations  14 us (1%)
    all_gather x1, waiting for transfers between devices, body(): key_part = lax.all_gather(local_keys, 'seq', axis=0, tiled=True)  197 us
    all_gather x1, waiting for transfers between devices, body(): value_part = lax.all_gather(local_values, 'seq', axis=0, tiled=True)  151 us
    dot_general x34, matrix products, absorb_block(): jnp.einsum('qhd,khd->hqk', query_heads, key_heads, preferred_element_type...  128 us
    dot_general x34, matrix products, absorb_block(): jnp.einsum('hqk,khd->qhd', weights.astype(jnp.bfloat16), value_heads, pre...  123 us
    all_gather x1, waiting for transfers between devices, body(): lax.all_gather(head_w1, 'type', axis=0, tiled=True)  109 us
    unnamed x22, local copies, waits for them, and re-layouts  51.3 us
    reduce_sum x34, other arithmetic, absorb_block(): totals = totals * decay + jnp.sum(weights, axis=-1)  43.5 us
    reshape x1, local copies, waits for them, and re-layouts, body(): key_blocks = key_part.reshape(row_total // 512, 512, local_heads, HD)  25.9 us
  transfers between devices with their start and end apart: 5, of which 5 were waited for; matrix products, arithmetic and copies ran while one was open for 6% of the time, Pallas kernels for 0%

commit v1 on v0

--- a/solution.py
+++ b/solution.py
@@ -64,8 +64,10 @@
         jnp.zeros((query_count, local_heads, HD), jnp.float32),
     )
     running = initial
-    key_part = lax.all_gather(local_keys, "seq", axis=0, tiled=True)
-    value_part = lax.all_gather(local_values, "seq", axis=0, tiled=True)
+    seen_now = lax.all_gather(
+        jnp.concatenate([local_keys, local_values], 1), "seq", axis=0, tiled=True
+    )
+    key_part, value_part = jnp.split(seen_now, [local_keys.shape[1]], 1)
     row_total = key_part.shape[0]
     key_blocks = key_part.reshape(row_total // 512, 512, local_heads, HD)
     value_blocks = value_part.reshape(row_total // 512, 512, local_heads, HD)

time: 962 us -> 1010 us (1.050)
  waiting for transfers between devices: 503 us -> 540 us
  local copies, waits for them, and re-layouts: 106 us -> 117 us
    all_gather x2 -> x1, waiting for transfers between devices: 347 us -> 383 us  [body(): lax.all_gather(jnp.concatenate([local_keys, local_values], 1), 'seq', axi...]
    split x0 -> x1, local copies, waits for them, and re-layouts: none -> 12 us  [body(): key_part, value_part = jnp.split(seen_now, [local_keys.shape[1]], 1)]
  transfers between devices with their start and end apart: 5 -> 4, of which waited for: 5 -> 4; matrix products, arithmetic and copies ran while one was open for 6% -> 0% of each run, Pallas kernels for 0% -> 0%
where the time goes in v1:
time: 1010 us; the launch traced here: 1000 us
  waiting for transfers between devices  540 us (53%)
  matrix products  265 us (26%)
  local copies, waits for them, and re-layouts  117 us (12%)
  other arithmetic  51.2 us (5%)
  blocking collectives  14.7 us (1%)
  between operations  14 us (1%)
    all_gather x1, waiting for transfers between devices, body(): lax.all_gather(jnp.concatenate([local_keys, local_values], 1), 'seq', axi...  383 us
    dot_general x34, matrix products, absorb_block(): jnp.einsum('qhd,khd->hqk', query_heads, key_heads, preferred_element_type...  129 us
    dot_general x34, matrix products, absorb_block(): jnp.einsum('hqk,khd->qhd', weights.astype(jnp.bfloat16), value_heads, pre...  123 us
    all_gather x1, waiting for transfers between devices, body(): lax.all_gather(head_w1, 'type', axis=0, tiled=True)  109 us
    unnamed x22, local copies, waits for them, and re-layouts  51.3 us
    reduce_sum x34, other arithmetic, absorb_block(): totals = totals * decay + jnp.sum(weights, axis=-1)  43.5 us
    reshape x1, local copies, waits for them, and re-layouts, body(): key_blocks = key_part.reshape(row_total // 512, 512, local_heads, HD)  25.9 us
    reshape x1, local copies, waits for them, and re-layouts, body(): value_blocks = value_part.reshape(row_total // 512, 512, local_heads, HD)  25.9 us
  transfers between devices with their start and end apart: 4, of which 4 were waited for; matrix products, arithmetic and copies ran while one was open for 0% of the time, Pallas kernels for 0%

profile of v1, /device:TPU:1, one launch (start us, length us, event | category | flops | bytes accessed | tf_op | source)
XLA Modules:
  0.0 1003.3 jit_solution(5186947992666180060)
XLA Ops:
  11.1 24.9 %all-gather.5.cloned.1.call-done = bf16[544,1024]{1,0:T(8,128)(2,1)} async-done(((bf16[136,1024]{1,0:T(8,128)(2,1)}), bf16[544,1024]{1,0:T(8,128)(2,1)}) %all-gather.5.cloned.1.call-update) | async-done | bytes 1114128 | tf_op jit(solution)/shard_map/all_gather | solution.py:50
  39.4 382.9 %all-gather.7.cloned.1.call-done = bf16[17408,512]{1,0:T(8,128)(2,1)} async-done(((bf16[544,512]{1,0:T(8,128)(2,1)}), bf16[17408,512]{1,0:T(8,128)(2,1)}) %all-gather.7.cloned.1.call-update) | async-done | bytes 17825808 | tf_op jit(solution)/shard_map/all_gather | solution.py:67
  422.3 12.0 %fusion.60 = (bf16[17408,256]{1,0:T(8,128)(2,1)}, bf16[17408,256]{1,0:T(8,128)(2,1)}) fusion(bf16[17408,512]{1,0:T(8,128)(2,1)} %all-gather.7.cloned.1.call-done), kind=kLoop, calls=%fused_computation.84 | loop fusion | bytes 35651584 | tf_op jit(solution)/shard_map/split | solution.py:70
  434.3 25.9 %reshape.73 = bf16[34,512,4,64]{3,2,1,0:T(4,128)(2,1)} reshape(bf16[17408,256]{1,0:T(8,128)(2,1)} %get-tuple-element.108) | data formatting | bytes 17825792 | tf_op jit(solution)/shard_map/reshape | solution.py:72
  460.2 25.6 %copy.24 = bf16[34,512,4,64]{1,3,2,0:T(8,128)(2,1)} copy(bf16[34,512,4,64]{3,2,1,0:T(4,128)(2,1)} %reshape.73) | data formatting | bytes 17825792
  485.8 25.9 %reshape.74 = bf16[34,512,4,64]{3,2,1,0:T(4,128)(2,1)} reshape(bf16[17408,256]{1,0:T(8,128)(2,1)} %get-tuple-element.107) | data formatting | bytes 17825792 | tf_op jit(solution)/shard_map/reshape | solution.py:73
  511.7 25.6 %copy.25 = bf16[34,512,4,64]{1,3,2,0:T(8,128)(2,1)} copy(bf16[34,512,4,64]{3,2,1,0:T(4,128)(2,1)} %reshape.74) | data formatting | bytes 17825792
  537.3 299.0 %while.15 = (s32[]{:T(128)}, f32[4,544]{1,0:T(4,128)S(1)}, f32[4,544]{1,0:T(4,128)S(1)}, f32[544,4,64]{0,2,1:T(8,128)S(1)}, bf16[34,512,4,64]{1,3,2,0:T(8,128)(2...) while((s32[]{:T(128)}, f32[4,544]{1,0:T(4,128)S(1)}, ...), condition=%wide.region_4.5_spmd.clone, body=%wide.region_1.4_spmd.clone.sunk | while | flops 294556416 | bytes 33252484 | solution.py:78
  537.3 3.8 bitcast_reduce_fusion.2
  546.2 3.8 bitcast_reduce_fusion.2
  563.8 3.8 bitcast_reduce_fusion.2
  572.5 3.8 bitcast_reduce_fusion.2
  616.5 3.8 bitcast_reduce_fusion.2
  634.1 3.8 bitcast_reduce_fusion.2
  651.7 3.8 bitcast_reduce_fusion.2
  669.3 3.8 bitcast_reduce_fusion.2
  686.8 3.8 bitcast_reduce_fusion.2
  704.4 3.8 bitcast_reduce_fusion.2
  774.8 3.8 bitcast_reduce_fusion.2
  839.8 7.3 all-gather
  847.1 7.4 all_gather.19
  854.6 22.1 %reduce-scatter.2.cloned.1.call-done = f32[136,1024]{1,0:T(8,128)} async-done(((f32[544,1024]{1,0:T(8,128)}), f32[136,1024]{1,0:T(8,128)}) %reduce-scatter.2.cloned.1.call-update) | async-done | bytes 557072 | tf_op jit(solution)/shard_map/reduce_scatter | solution.py:83
  878.7 109.4 %all-gather.9.cloned.1.call-done = bf16[8,1024,1024]{2,1,0:T(8,128)(2,1)} async-done(((bf16[2,1024,1024]{2,1,0:T(8,128)(2,1)}), bf16[8,1024,1024]{2,1,0:T(8,128)(2,1)}) %all-gather.9.cloned.1.call-update) | async-done | bytes 16777232 | tf_op jit(solution)/shard_map/all_gather | solution.py:104
  988.2 7.6 fusion.32
  (320 shorter events, 269.8 us)
Async XLA Ops:
  7.2 28.8 %copy-start = (bf16[3,1024,256]{2,1,0:T(8,128)(2,1)S(1)}, bf16[3,1024,256]{2,1,0:T(8,128)(2,1)}, u32[]{:S(2)}) copy-start(bf16[3,1024,256]{2,1,0:T(8,128)(2,1)} %param.16) | copy-start | bytes 4718596
  7.2 28.7 %all-gather.5.cloned.1.call-start = ((), (), s32[]{:S(2)}) async-start(), calls=%async_computation.1 | async-start | bytes 1392640 | tf_op jit(solution)/shard_map/all_gather | solution.py:50
  11.0 411.3 %all-gather.7.cloned.1.call-start = ((), (), s32[]{:S(2)}) async-start(), calls=%async_computation.2 | async-start | bytes 18382848 | tf_op jit(solution)/shard_map/all_gather | solution.py:67
  39.2 837.5 %reduce-scatter.2.cloned.1.call-start = ((), (), s32[]{:S(2)}) async-start(), calls=%async_computation.3 | async-start | bytes 2785280 | tf_op jit(solution)/shard_map/reduce_scatter | solution.py:83
  537.3 299.0 %copy-start.5 = (bf16[256,1024]{1,0:T(8,128)(2,1)S(1)}, bf16[256,1024]{1,0:T(8,128)(2,1)}, u32[]{:S(2)}) copy-start(bf16[256,1024]{1,0:T(8,128)(2,1)} %param.17) | copy-start | bytes 1572868
  550.0 3.7 copy-start.2
  558.7 3.7 copy-start.2
  576.3 3.7 copy-start.2
  593.9 3.7 copy-start.2
  602.7 3.7 copy-start.2
  620.3 3.7 copy-start.2
  637.9 3.7 copy-start.2
  717.0 3.7 copy-start.2
  734.6 3.7 copy-start.2
  752.2 3.7 copy-start.2
  778.5 3.7 copy-start.2
  796.1 3.7 copy-start.2
  836.4 10.7 %copy-start.6 = (bf16[2,1024,16]{1,2,0:T(8,128)(2,1)S(1)}, bf16[2,1024,16]{1,2,0:T(8,128)(2,1)}, u32[]{:S(2)}) copy-start(bf16[2,1024,16]{1,2,0:T(8,128)(2,1)} %param.21) | copy-start | bytes 196612
  836.4 40.3 %copy-start.3 = (bf16[136,1024]{1,0:T(8,128)(2,1)S(1)}, bf16[136,1024]{1,0:T(8,128)(2,1)}, u32[]{:S(2)}) copy-start(bf16[136,1024]{1,0:T(8,128)(2,1)} %param.12) | copy-start | bytes 835588
  836.4 40.3 %copy-start.8 = (f32[1024]{0:T(1024)S(1)}, f32[1024]{0:T(1024)}, u32[]{:S(2)}) copy-start(f32[1024]{0:T(1024)} %param.14) | copy-start | bytes 12292
  838.3 39.7 %copy-start.9 = (f32[1024]{0:T(1024)S(1)}, f32[1024]{0:T(1024)}, u32[]{:S(2)}) copy-start(f32[1024]{0:T(1024)} %param.15) | copy-start | bytes 12292
  838.3 149.9 %all-gather.9.cloned.1.call-start = ((), (), s32[]{:S(2)}) async-start(), calls=%async_computation.4 | async-start | bytes 20971520 | tf_op jit(solution)/shard_map/all_gather | solution.py:104
  877.9 117.8 %copy-start.4 = (bf16[136,1024]{1,0:T(8,128)(2,1)}, bf16[136,1024]{1,0:T(8,128)(2,1)S(1)}, u32[]{:S(2)}) copy-start(bf16[136,1024]{1,0:T(8,128)(2,1)S(1)} %get-tuple-element.104) | copy-start | bytes 835588
  988.2 8.6 copy-start.1
  (24 other events, 86.9 us)
Sparse Core Ops, SparseCore 0:
  11.1 24.7 all-gather.4
  39.3 382.9 all-gather.6
  838.4 38.2 reduce-scatter.1
  878.3 109.7 all-gather.8
